TPU v7x, 512 devices: a whole 4x8x8 slice. The times are simulated.
512 devices in a mesh: seq: 128 (over y, z, core), tp: 4 (over x).
Axes of the slice: x: 4, y: 8, z: 8, core: 2. Of those that a mesh axis runs over, the one named last changes fastest.
Arguments:
- tokens: bfloat16 [32768, 1280], P('seq', 'tp'), may hold values from -6 to 6
- first_gain: float32 [1280], replicated, may hold values from 0.1 to 1.9
- w_query: bfloat16 [1280, 1280], P(None, 'tp')
- w_key: bfloat16 [1280, 1280], P(None, 'tp')
- w_value: bfloat16 [1280, 1280], P(None, 'tp'), may hold values from -0.15625 to 0.15625
- w_out: bfloat16 [1280, 1280], P('tp'), may hold values from -0.625 to 0.625
- segment_ids: int32 [32768], P('seq'), may hold values from 0 to 191, never falling along the last dimension, each value on 1 to 512 neighbouring positions
- keep_mask: int32 [32768], P('seq'), may hold values 0 or 1
- merge_gain: float32 [1280], replicated, may hold values from 0.1 to 1.9
- w_merge: bfloat16 [5120, 640], P('tp'), may hold values from -0.078125 to 0.078125
- merge_index: int32 [8192, 4], P('seq'), may hold values from 0 to 32767, as said below
- destination: int32 [8192], P('seq'), may hold values from 0 to 8191, as said below
Outputs:
- delivered: bfloat16 [8192, 640], P('seq', 'tp')
Inputs may be any that keep to these rules, and one draw needn't show every extreme that they name: `segment_ids`: segment numbers never fall along the tokens; each picture or clip holds 1 to 512 tokens and one holds exactly 512. `merge_index`: the four entries of merged row m are different tokens of the device that holds row m, that is of rows (m // 64) * 256 to that plus 256 - 1; every token lies in exactly one group. `destination`: a permutation of the merged rows. The owner of row m is destination[m] // 64; the 64 rows of each device go to exactly 32 owners, exactly 2 rows to each.
All inputs are finite; a program needn't handle non-finite values. No bound on the sum of `keep_mask` on one device may be relied on, other than what follows from the above.
Results may differ from a plain program's by a relative error of at most 0.022.
Values may be sent and summed in bfloat16 or wider, within the bound.
No kernel may reach another device: no remote copies, remote signals or barrier semaphores. Data moves between devices by JAX's collectives and lax.ppermute only.
A program may use at most 64 MiB of HBM per device.

v0:
```python
import jax
import jax.numpy as jnp
from jax import lax
from jax.sharding import PartitionSpec as P

HD = 80
EPS = 1e-06


def from_behind(shard, axis, by):
    length = lax.axis_size(axis)
    pairs = [(i, i + by) for i in range(length) if 0 <= i + by < length]
    return lax.ppermute(shard, axis, pairs)


def layer_norm(activations, norm_gain):
    activations = activations.astype(jnp.float32)
    row_mean = jnp.mean(activations, axis=-1, keepdims=True)
    centered = activations - row_mean
    variance = jnp.mean(centered * centered, axis=-1, keepdims=True)
    return centered * lax.rsqrt(variance + EPS) * norm_gain


def body(
    tokens,
    first_gain,
    w_query,
    w_key,
    w_value,
    w_out,
    segment_ids,
    keep_mask,
    merge_gain,
    w_merge,
    merge_index,
    destination,
):
    row_count = tokens.shape[0]
    local_width = w_query.shape[1]
    heads_here = local_width // HD
    gathered = lax.all_gather(tokens, "tp", axis=1, tiled=True)
    normed = layer_norm(gathered, first_gain).astype(jnp.bfloat16)
    queries = jnp.dot(normed, w_query, preferred_element_type=jnp.float32).astype(jnp.bfloat16)
    key_rows = jnp.dot(normed, w_key, preferred_element_type=jnp.float32).astype(jnp.bfloat16)
    value_rows = jnp.dot(normed, w_value, preferred_element_type=jnp.float32).astype(jnp.bfloat16)
    paired = jnp.concatenate([key_rows, value_rows], axis=1)
    code_query = segment_ids + 1
    code_key = jnp.where(keep_mask > 0, code_query, 0)
    pair_list = [paired]
    code_list = [code_key]
    for offset in (1, 2, -1, -2):
        moved_pair, moved_code = from_behind((paired, code_key), "seq", offset)
        pair_list.append(moved_pair)
        code_list.append(moved_code)
    all_pairs = jnp.concatenate(pair_list, axis=0)
    all_codes = jnp.concatenate(code_list, axis=0)
    window = all_pairs.shape[0]
    key_heads = all_pairs[:, :local_width].reshape(window, heads_here, HD)
    value_heads = all_pairs[:, local_width:].reshape(window, heads_here, HD)
    query_heads = queries.reshape(row_count, heads_here, HD)
    score_scale = HD ** (-0.5)
    scores = (
        jnp.einsum("qhd,khd->hqk", query_heads, key_heads, preferred_element_type=jnp.float32)
        * score_scale
    )
    query_pos = jnp.arange(row_count)[:, None]
    key_pos = jnp.arange(window)[None, :]
    allowed = (code_query[:, None] == all_codes[None, :]) | (key_pos == query_pos)
    scores = jnp.where(allowed[None], scores, -1e30)
    row_max = jnp.max(scores, axis=-1, keepdims=True)
    exponent = jnp.exp(scores - row_max)
    row_total = jnp.sum(exponent, axis=-1, keepdims=True)
    weights = (exponent / row_total).astype(jnp.bfloat16)
    attended = jnp.einsum("hqk,khd->qhd", weights, value_heads, preferred_element_type=jnp.float32)
    attended = attended.reshape(row_count, local_width).astype(jnp.bfloat16)
    partial_sum = jnp.dot(attended, w_out, preferred_element_type=jnp.float32)
    position = lax.axis_index("tp")
    seq_index = lax.axis_index("seq")
    local_index = merge_index - seq_index * row_count
    column = lax.dynamic_slice_in_dim(local_index, position, 1, 1)[:, 0]
    mixed_sum = lax.psum(partial_sum.astype(jnp.bfloat16), "tp").astype(jnp.float32)
    updated = gathered.astype(jnp.float32) + mixed_sum
    merged_norm = layer_norm(updated, merge_gain).astype(jnp.bfloat16)
    picked = jnp.take(merged_norm, column, axis=0)
    partial_proj = jnp.dot(picked, w_merge, preferred_element_type=jnp.float32)
    projected = lax.psum_scatter(
        partial_proj.astype(jnp.bfloat16), "tp", scatter_dimension=1, tiled=True
    )
    slot_count = projected.shape[0]
    slot_range = jnp.arange(slot_count)
    piece_rows = lax.all_gather(projected, "seq", axis=0, tiled=True)
    piece_dest = lax.all_gather(destination, "seq", axis=0, tiled=True)
    piece_slot = piece_dest - seq_index * slot_count
    one_hot = (piece_slot[None, :] == slot_range[:, None]).astype(jnp.bfloat16)
    delivered = jnp.dot(one_hot, piece_rows, preferred_element_type=jnp.float32)
    return delivered.astype(jnp.bfloat16)


def solution(mesh):
    return jax.shard_map(
        body,
        mesh=mesh,
        in_specs=(
            P("seq", "tp"),
            P(),
            P(None, "tp"),
            P(None, "tp"),
            P(None, "tp"),
            P("tp", None),
            P("seq"),
            P("seq"),
            P(),
            P("tp", None),
            P("seq", None),
            P("seq"),
        ),
        out_specs=P("seq", "tp"),
        check_vma=False,
    )
```

profile of v0, /device:TPU:2, one launch (start us, length us, event | category | flops | bytes accessed | tf_op | source)
XLA Modules:
  0.0 674.0 jit_solution(445219230451714577)
XLA Ops:
  6.5 0.0 copy-start
  6.5 0.0 all-reduce.3.cloned.1.call-start
  6.5 16.1 %all_gather.10 = bf16[256,1280]{0,1:T(8,128)(2,1)S(1)} all-gather(bf16[256,320]{0,1:T(8,128)(2,1)} %param.12), channel_id=1, replica_groups=mesh['seq'=128,'tp'=4] {'tp'}, dimensions={1}, use_global_device_ids=true | all-gather | bytes 819200 | tf_op jit(solution)/shard_map/all_gather | solution.py:41
  22.6 0.2 copy.14
  22.9 0.0 copy-start.10
  22.9 0.2 convert_reduce_fusion
  23.1 0.3 fusion.10
  23.4 0.0 copy-start.11
  23.4 0.0 copy-done.12
  23.4 0.6 copy-done.10
  24.0 0.5 convolution_convert_fusion.3
  24.6 0.0 copy-done.11
  24.6 0.5 convolution_convert_fusion.2
  25.1 1.0 pad_maximum_fusion
  26.1 2.0 collective-permute-start
  28.1 2.2 collective-permute-start.1
  30.3 1.3 collective-permute-start.2
  31.6 1.3 collective-permute-start.3
  32.9 0.0 copy-done.8
  32.9 0.0 copy-done.9
  32.9 0.0 copy-start.2
  32.9 4.9 collective-permute-start.4
  37.8 2.3 convolution_convert_fusion.1
  40.2 0.0 collective-permute-done.4
  40.2 4.9 collective-permute-start.5
  45.0 1.3 collective-permute-done.5
  46.3 1.3 collective-permute-start.6
  47.6 2.1 collective-permute-done.6
  49.7 1.3 collective-permute-start.7
  51.0 5.7 collective-permute-done.7
  56.8 1.0 fusion.13
  57.8 0.0 collective-permute-done
  57.8 1.0 constant_dynamic-update-slice_fusion.3
  58.8 0.0 collective-permute-done.1
  58.8 0.0 collective-permute-done.2
  58.9 0.0 collective-permute-done.3
  58.9 1.0 fusion.35
  59.9 3.1 exponential_reduce_fusion
  63.1 0.0 copy-start.3
  63.1 4.5 fusion.16
  67.6 0.0 copy-done.3
  67.6 2.3 convolution_convert_fusion
  69.9 0.0 all-reduce.3.cloned.1.call-update
  69.9 0.0 reduce-scatter.4.cloned.1.call-start
  70.0 0.0 copy-start.6
  70.0 65.5 %all-reduce.3.cloned.1.call-done = bf16[256,1280]{1,0:T(8,128)(2,1)} async-done(((bf16[256,1280]{1,0:T(8,128)(2,1)}), bf16[256,1280]{1,0:T(8,128)(2,1)}) %all-reduce.3.cloned.1.call-update) | async-done | bytes 655376 | tf_op jit(solution)/shard_map/psum | solution.py:81
  135.6 1.4 fusion.15
  137.0 0.3 multiply_reduce_fusion
  137.4 0.0 copy-done.6
  137.4 0.3 multiply_convert_fusion
  137.7 0.7 gather_fusion
  138.4 0.0 copy-start.13
  138.4 0.0 copy-done
  138.4 0.5 convolution_convert_fusion.4
  138.9 0.8 copy.15
  139.7 0.0 reduce-scatter.4.cloned.1.call-update
  139.7 0.0 all-gather.2.cloned.1.call-start
  139.8 26.4 %reduce-scatter.4.cloned.1.call-done = bf16[160,64]{1,0:T(8,128)(2,1)} async-done(((bf16[640,64]{1,0:T(8,128)(2,1)}), bf16[160,64]{1,0:T(8,128)(2,1)}) %reduce-scatter.4.cloned.1.call-update) | async-done | bytes 20496
  166.1 1.5 copy.16
  167.6 0.0 all-gather.2.cloned.1.call-update
  167.6 1.3 dynamic-slice
  169.6 0.3 dynamic-update-slice
  169.9 494.1 %all-reduce = s32[8192]{0:T(1024)S(1)} all-reduce(s32[8192]{0:T(1024)S(1)} %dynamic-update-slice), channel_id=1, replica_groups=mesh['seq'=128,'tp'=4] {'seq'}, use_global_device_ids=true, to_apply=%add | all-reduce | flops 8192 | bytes 65536
  664.0 3.5 fusion.17
  (32 shorter events, 0.2 us)
Async XLA Ops:
  6.5 131.9 %copy-start = (bf16[1280,640]{1,0:T(8,128)(2,1)S(1)}, bf16[1280,640]{1,0:T(8,128)(2,1)}, u32[]{:S(2)}) copy-start(bf16[1280,640]{1,0:T(8,128)(2,1)} %param.21) | copy-start | bytes 4915204
  6.5 129.0 %all-reduce.3.cloned.1.call-start = ((), (), s32[]{:S(2)}) async-start(), calls=%async_computation.1 | async-start | bytes 1310720 | tf_op jit(solution)/shard_map/psum | solution.py:81
  22.6 0.8 copy-start.12
  22.9 1.1 copy-start.10
  23.4 1.2 copy-start.11
  24.6 8.3 %copy-start.8 = (s32[256]{0:T(256)S(1)}, s32[256]{0:T(256)}, u32[]{:S(2)}) copy-start(s32[256]{0:T(256)} %param.18) | copy-start | bytes 3076
  24.6 8.3 %copy-start.9 = (s32[256]{0:T(256)S(1)}, s32[256]{0:T(256)}, u32[]{:S(2)}) copy-start(s32[256]{0:T(256)} %param.19) | copy-start | bytes 3076
  26.1 31.7 %collective-permute-start = (bf16[256,640]{0,1:T(8,128)(2,1)}, bf16[256,640]{0,1:T(8,128)(2,1)}, u32[]{:S(2)}, u32[]{:S(2)}) collective-permute-start(bf16[256,640]{0,1:T(8,128)(2,1)} %get-tuple-element.11), channel_id=1, source_target_pairs={{0,4},{4,8},{8,12},{12,16},{16,20},{20,24},{24,28},{28,32},{32,36}... | collective-permute-start | bytes 983048 | tf_op jit(solution)/shard_map/ppermute | solution.py:13
  28.1 30.7 %collective-permute-start.1 = (bf16[256,640]{0,1:T(8,128)(2,1)}, bf16[256,640]{0,1:T(8,128)(2,1)S(1)}, u32[]{:S(2)}, u32[]{:S(2)}) collective-permute-start(bf16[256,640]{0,1:T(8,128)(2,1)} %get-tuple-element.11), channel_id=1, source_target_pairs={{0,8},{4,12},{8,16},{12,20},{16,24},{20,28},{24,32},{28,36},{32,40... | collective-permute-start | bytes 983048 | tf_op jit(solution)/shard_map/ppermute | solution.py:13
  30.3 28.5 %collective-permute-start.2 = (bf16[256,640]{0,1:T(8,128)(2,1)}, bf16[256,640]{0,1:T(8,128)(2,1)S(1)}, u32[]{:S(2)}, u32[]{:S(2)}) collective-permute-start(bf16[256,640]{0,1:T(8,128)(2,1)} %get-tuple-element.11), channel_id=1, source_target_pairs={{4,0},{8,4},{12,8},{16,12},{20,16},{24,20},{28,24},{32,28},{36,32}... | collective-permute-start | bytes 983048 | tf_op jit(solution)/shard_map/ppermute | solution.py:13
  31.6 27.3 %collective-permute-start.3 = (bf16[256,640]{0,1:T(8,128)(2,1)}, bf16[256,640]{0,1:T(8,128)(2,1)S(1)}, u32[]{:S(2)}, u32[]{:S(2)}) collective-permute-start(bf16[256,640]{0,1:T(8,128)(2,1)} %get-tuple-element.11), channel_id=1, source_target_pairs={{8,0},{12,4},{16,8},{20,12},{24,16},{28,20},{32,24},{36,28},{40,32... | collective-permute-start | bytes 983048 | tf_op jit(solution)/shard_map/ppermute | solution.py:13
  32.9 24.9 %copy-start.2 = (bf16[1280,640]{0,1:T(8,128)(2,1)S(1)}, bf16[1280,640]{0,1:T(8,128)(2,1)}, u32[]{:S(2)}) copy-start(bf16[1280,640]{0,1:T(8,128)(2,1)} %get-tuple-element.12) | copy-start | bytes 4915204
  32.9 7.2 %collective-permute-start.4 = (s32[256]{0:T(256)S(1)}, s32[256]{0:T(256)S(1)}, u32[]{:S(2)}, u32[]{:S(2)}) collective-permute-start(s32[256]{0:T(256)S(1)} %get-tuple-element.8), channel_id=1, source_target_pairs={{0,4},{4,8},{8,12},{12,16},{16,20},{20,24},{24,28},{28,32},{32,36}... | collective-permute-start | bytes 3080 | tf_op jit(solution)/shard_map/ppermute | solution.py:13
  40.2 6.1 collective-permute-start.5
  46.3 3.4 collective-permute-start.6
  49.7 7.0 %collective-permute-start.7 = (s32[256]{0:T(256)S(1)}, s32[256]{0:T(256)S(1)}, u32[]{:S(2)}, u32[]{:S(2)}) collective-permute-start(s32[256]{0:T(256)S(1)} %get-tuple-element.8), channel_id=1, source_target_pairs={{8,0},{12,4},{16,8},{20,12},{24,16},{28,20},{32,24},{36,28},{40,32... | collective-permute-start | bytes 3080 | tf_op jit(solution)/shard_map/ppermute | solution.py:13
  58.9 1.0 copy-start.5
  59.9 3.1 copy-start.4
  63.1 4.5 copy-start.3
  67.6 2.4 copy-start.7
  69.9 96.2 %reduce-scatter.4.cloned.1.call-start = ((), (), s32[]{:S(2)}) async-start(), calls=%async_computation.3 | async-start | bytes 204800
  70.0 67.3 %copy-start.6 = (f32[1280]{0:T(1024)S(1)}, f32[1280]{0:T(1024)}, u32[]{:S(2)}) copy-start(f32[1280]{0:T(1024)} %param.20) | copy-start | bytes 15364
  135.6 1.4 copy-start.1
  138.4 31.2 %copy-start.13 = (s32[64]{0:T(128)S(1)}, s32[64]{0:T(128)}, u32[]{:S(2)}) copy-start(s32[64]{0:T(128)} %param.23) | copy-start | bytes 772
  139.7 524.2 %all-gather.2.cloned.1.call-start = ((), (), s32[]{:S(2)}) async-start(), calls=%async_computation.2 | async-start | bytes 4227072 | tf_op jit(solution)/shard_map/all_gather | solution.py:91
Sparse Core Ops, SparseCore 0:
  70.0 65.4 all-reduce.2
  139.8 26.2 reduce-scatter.3
  169.3 85.4 all-gather.1
where the time goes:
time: 675 us; the launch traced here: 674 us
  blocking collectives  510 us (76%)
  waiting for transfers between devices  101 us (15%)
  starting transfers between devices  19.1 us (3%)
  matrix products  17.3 us (3%)
  between operations  14.1 us (2%)
  local copies, waits for them, and re-layouts  7.64 us (1%)
    unnamed x1, blocking collectives  494 us
    psum x1, waiting for transfers between devices, body(): lax.psum(partial_sum.astype(jnp.bfloat16), 'tp').astype(jnp.float32)  65.5 us
    unnamed x4, waiting for transfers between devices  26.4 us
    ppermute x8, starting transfers between devices, from_behind(): return lax.ppermute(shard, axis, pairs)  19.1 us
    all_gather x1, blocking collectives, body(): gathered = lax.all_gather(tokens, 'tp', axis=1, tiled=True)  16.1 us
  transfers between devices with their start and end apart: 11, of which 5 were waited for; matrix products, arithmetic and copies ran while one was open for 1% of the time, Pallas kernels for 0%

commit v1 on v0

--- a/solution.py
+++ b/solution.py
@@ -38,7 +38,9 @@
     row_count = tokens.shape[0]
     local_width = w_query.shape[1]
     heads_here = local_width // HD
-    gathered = lax.all_gather(tokens, "tp", axis=1, tiled=True)
+    gathered = jnp.concatenate(
+        lax.all_to_all(jnp.stack([tokens] * lax.axis_size("tp")), "tp", 0, 0), axis=1
+    )
     normed = layer_norm(gathered, first_gain).astype(jnp.bfloat16)
     queries = jnp.dot(normed, w_query, preferred_element_type=jnp.float32).astype(jnp.bfloat16)
     key_rows = jnp.dot(normed, w_key, preferred_element_type=jnp.float32).astype(jnp.bfloat16)

time: 675 us -> 664 us (0.984)
  blocking collectives: 510 us -> 494 us
    all_gather x1 -> x0, blocking collectives: 16.1 us -> none  [body(): gathered = lax.all_gather(tokens, 'tp', axis=1, tiled=True)]
    psum x1, waiting for transfers between devices: 65.5 us -> 52 us  [body(): lax.psum(partial_sum.astype(jnp.bfloat16), 'tp').astype(jnp.float32)]
    ppermute x8, waiting for transfers between devices: 9.14 us -> 19.8 us  [from_behind(): return lax.ppermute(shard, axis, pairs)]
    all_to_all x0 -> x1, starting transfers between devices: none -> 9.33 us  [body(): lax.all_to_all(jnp.stack([tokens] * lax.axis_size('tp')), 'tp', 0, 0)]
  transfers between devices with their start and end apart: 11 -> 12, of which waited for: 5 -> 6; matrix products, arithmetic and copies ran while one was open for 1% -> 1% of each run, Pallas kernels for 0% -> 0%
where the time goes in v1:
time: 664 us; the launch traced here: 663 us
  blocking collectives  494 us (74%)
  waiting for transfers between devices  98.2 us (15%)
  starting transfers between devices  24.6 us (4%)
  matrix products  15.8 us (2%)
  between operations  14.1 us (2%)
  local copies, waits for them, and re-layouts  11.1 us (2%)
    unnamed x1, blocking collectives  494 us
    psum x1, waiting for transfers between devices, body(): lax.psum(partial_sum.astype(jnp.bfloat16), 'tp').astype(jnp.float32)  52 us
    unnamed x4, waiting for transfers between devices  26.4 us
    ppermute x8, waiting for transfers between devices, from_behind(): return lax.ppermute(shard, axis, pairs)  19.8 us
    ppermute x8, starting transfers between devices, from_behind(): return lax.ppermute(shard, axis, pairs)  15.2 us
  transfers between devices with their start and end apart: 12, of which 6 were waited for; matrix products, arithmetic and copies ran while one was open for 1% of the time, Pallas kernels for 0%

profile of v1, /device:TPU:2, one launch (start us, length us, event | category | flops | bytes accessed | tf_op | source)
XLA Modules:
  0.0 663.0 jit_solution(6816031242047209145)
XLA Ops:
  6.5 0.0 copy-start
  6.5 1.9 stack.2
  8.5 9.3 %all-to-all-start = ((bf16[4,256,320]{1,2,0:T(8,128)(2,1)}), bf16[4,256,320]{1,2,0:T(8,128)(2,1)S(1)}, u32[]{:S(2)}, u32[]{:S(2)}) async-start(bf16[4,256,320]{1,2,0:T(8,128)(2,1)} %stack.2), calls=%async_computation | async-start | bytes 1310720 | tf_op jit(solution)/shard_map/all_to_all | solution.py:42
  17.8 0.0 all-reduce.3.cloned.1.call-start
  17.8 0.0 copy-done.10
  17.8 0.0 copy-done.11
  17.8 1.4 collective-permute-start.4
  19.3 1.3 collective-permute-start.5
  20.6 1.3 collective-permute-start.6
  21.9 1.3 collective-permute-start.7
  23.2 0.0 collective-permute-done.4
  23.2 0.0 collective-permute-done.5
  23.2 1.2 collective-permute-done.6
  24.4 4.4 collective-permute-done.7
  28.9 0.0 all-to-all-done
  28.9 0.2 convert_reduce_fusion
  29.1 0.2 multiply_reduce_fusion.1
  29.3 0.0 copy-done.7
  29.3 0.2 multiply_convert_fusion.1
  29.6 0.0 copy-done.2
  29.6 0.4 convolution_convert_fusion.2
  30.0 0.5 copy-done.3
  30.4 0.4 convolution_convert_fusion.3
  30.9 2.0 collective-permute-start
  32.9 0.2 fusion.8
  33.2 5.3 collective-permute-start.1
  38.5 1.3 collective-permute-start.2
  39.8 1.3 collective-permute-start.3
  41.1 0.0 copy-done.4
  41.1 1.1 convolution_convert_fusion.1
  42.1 0.0 collective-permute-done
  42.2 2.7 collective-permute-done.1
  44.9 0.0 collective-permute-done.2
  45.0 11.4 %collective-permute-done.3 = bf16[256,640]{0,1:T(8,128)(2,1)S(1)} collective-permute-done((bf16[256,640]{0,1:T(8,128)(2,1)S(1)}, bf16[256,640]{0,1:T(8,128)(2,1)S(1)}, u32[]{:S(2)}, u32[]{:S(2)}) %collective-permute-start.3) | collective-permute-done | bytes 327712 | tf_op jit(solution)/shard_map/ppermute | solution.py:13
  56.4 1.0 fusion.26
  57.4 3.1 exponential_reduce_fusion
  60.5 0.0 copy-done.6
  60.5 0.0 copy-start.5
  60.6 4.5 fusion.9
  65.1 0.0 copy-done.5
  65.1 2.3 convolution_convert_fusion
  67.4 0.0 all-reduce.3.cloned.1.call-update
  67.4 0.0 reduce-scatter.4.cloned.1.call-start
  67.6 1.2 convert_element_type.73
  68.7 1.7 copy.15
  70.5 0.0 copy-start.8
  70.5 52.0 %all-reduce.3.cloned.1.call-done = bf16[256,1280]{1,0:T(8,128)(2,1)} async-done(((bf16[256,1280]{1,0:T(8,128)(2,1)}), bf16[256,1280]{1,0:T(8,128)(2,1)}) %all-reduce.3.cloned.1.call-update) | async-done | bytes 655376 | tf_op jit(solution)/shard_map/psum | solution.py:83
  122.5 1.4 fusion.14
  123.8 0.0 copy-done.1
  123.8 0.3 multiply_reduce_fusion
  124.2 1.1 multiply_convert_fusion
  125.4 2.0 gather_fusion
  127.4 0.0 copy-done
  127.4 0.5 convolution_convert_fusion.4
  127.9 0.8 copy.16
  128.7 0.0 reduce-scatter.4.cloned.1.call-update
  128.7 0.0 all-gather.2.cloned.1.call-start
  128.7 26.4 %reduce-scatter.4.cloned.1.call-done = bf16[160,64]{1,0:T(8,128)(2,1)} async-done(((bf16[640,64]{1,0:T(8,128)(2,1)}), bf16[160,64]{1,0:T(8,128)(2,1)}) %reduce-scatter.4.cloned.1.call-update) | async-done | bytes 20496
  155.1 1.5 copy.17
  156.6 0.0 all-gather.2.cloned.1.call-update
  156.6 1.3 dynamic-slice
  158.5 0.3 dynamic-update-slice
  158.8 494.2 %all-reduce = s32[8192]{0:T(1024)S(1)} all-reduce(s32[8192]{0:T(1024)S(1)} %dynamic-update-slice), channel_id=1, replica_groups=mesh['seq'=128,'tp'=4] {'seq'}, use_global_device_ids=true, to_apply=%add | all-reduce | flops 8192 | bytes 65536
  653.0 3.5 fusion.10
  (34 shorter events, 0.2 us)
Async XLA Ops:
  6.5 120.9 %copy-start = (bf16[1280,640]{1,0:T(8,128)(2,1)S(1)}, bf16[1280,640]{1,0:T(8,128)(2,1)}, u32[]{:S(2)}) copy-start(bf16[1280,640]{1,0:T(8,128)(2,1)} %param.21) | copy-start | bytes 4915204
  6.5 11.3 %copy-start.10 = (s32[256]{0:T(256)S(1)}, s32[256]{0:T(256)}, u32[]{:S(2)}) copy-start(s32[256]{0:T(256)} %param.18) | copy-start | bytes 3076
  6.5 11.3 %copy-start.11 = (s32[256]{0:T(256)S(1)}, s32[256]{0:T(256)}, u32[]{:S(2)}) copy-start(s32[256]{0:T(256)} %param.19) | copy-start | bytes 3076
  6.5 22.8 %copy-start.7 = (f32[1280]{0:T(1024)S(1)}, f32[1280]{0:T(1024)}, u32[]{:S(2)}) copy-start(f32[1280]{0:T(1024)} %param.13) | copy-start | bytes 15364
  8.5 20.4 %all-to-all-start = ((bf16[4,256,320]{1,2,0:T(8,128)(2,1)}), bf16[4,256,320]{1,2,0:T(8,128)(2,1)S(1)}, u32[]{:S(2)}, u32[]{:S(2)}) async-start(bf16[4,256,320]{1,2,0:T(8,128)(2,1)} %stack.2), calls=%async_computation | async-start | bytes 1310720 | tf_op jit(solution)/shard_map/all_to_all | solution.py:42
  17.8 11.8 %copy-start.2 = (bf16[1280,320]{0,1:T(8,128)(2,1)S(1)}, bf16[1280,320]{0,1:T(8,128)(2,1)}, u32[]{:S(2)}) copy-start(bf16[1280,320]{0,1:T(8,128)(2,1)} %param.16) | copy-start | bytes 2457604
  17.8 104.7 %all-reduce.3.cloned.1.call-start = ((), (), s32[]{:S(2)}) async-start(), calls=%async_computation.2 | async-start | bytes 1310720 | tf_op jit(solution)/shard_map/psum | solution.py:83
  17.8 5.3 collective-permute-start.4
  19.3 3.9 collective-permute-start.5
  20.6 3.9 collective-permute-start.6
  21.9 7.0 %collective-permute-start.7 = (s32[256]{0:T(256)S(1)}, s32[256]{0:T(256)S(1)}, u32[]{:S(2)}, u32[]{:S(2)}) collective-permute-start(s32[256]{0:T(256)S(1)} %get-tuple-element.8), channel_id=1, source_target_pairs={{8,0},{12,4},{16,8},{20,12},{24,16},{28,20},{32,24},{36,28},{40,32... | collective-permute-start | bytes 3080 | tf_op jit(solution)/shard_map/ppermute | solution.py:13
  29.3 1.1 copy-start.3
  30.4 10.6 %copy-start.4 = (bf16[1280,320]{0,1:T(8,128)(2,1)S(1)}, bf16[1280,320]{0,1:T(8,128)(2,1)}, u32[]{:S(2)}) copy-start(bf16[1280,320]{0,1:T(8,128)(2,1)} %param.14) | copy-start | bytes 2457604
  30.9 11.2 %collective-permute-start = (bf16[256,640]{0,1:T(8,128)(2,1)S(1)}, bf16[256,640]{0,1:T(8,128)(2,1)S(1)}, u32[]{:S(2)}, u32[]{:S(2)}) collective-permute-start(bf16[256,640]{0,1:T(8,128)(2,1)S(1)} %get-tuple-element.11), channel_id=1, source_target_pairs={{0,4},{4,8},{8,12},{12,16},{16,20},{20,24},{24,28},{28,32},{32,36}... | collective-permute-start | bytes 983048 | tf_op jit(solution)/shard_map/ppermute | solution.py:13
  33.2 11.7 %collective-permute-start.1 = (bf16[256,640]{0,1:T(8,128)(2,1)S(1)}, bf16[256,640]{0,1:T(8,128)(2,1)S(1)}, u32[]{:S(2)}, u32[]{:S(2)}) collective-permute-start(bf16[256,640]{0,1:T(8,128)(2,1)S(1)} %get-tuple-element.11), channel_id=1, source_target_pairs={{0,8},{4,12},{8,16},{12,20},{16,24},{20,28},{24,32},{28,36},{32,40... | collective-permute-start | bytes 983048 | tf_op jit(solution)/shard_map/ppermute | solution.py:13
  38.5 6.5 collective-permute-start.2
  39.8 16.6 %collective-permute-start.3 = (bf16[256,640]{0,1:T(8,128)(2,1)S(1)}, bf16[256,640]{0,1:T(8,128)(2,1)S(1)}, u32[]{:S(2)}, u32[]{:S(2)}) collective-permute-start(bf16[256,640]{0,1:T(8,128)(2,1)S(1)} %get-tuple-element.11), channel_id=1, source_target_pairs={{8,0},{12,4},{16,8},{20,12},{24,16},{28,20},{32,24},{36,28},{40,32... | collective-permute-start | bytes 983048 | tf_op jit(solution)/shard_map/ppermute | solution.py:13
  57.4 3.1 copy-start.6
  60.5 4.5 copy-start.5
  65.1 2.4 copy-start.9
  67.4 87.7 %reduce-scatter.4.cloned.1.call-start = ((), (), s32[]{:S(2)}) async-start(), calls=%async_computation.4 | async-start | bytes 204800
  70.5 53.7 %copy-start.8 = (f32[1280]{0:T(1024)S(1)}, f32[1280]{0:T(1024)}, u32[]{:S(2)}) copy-start(f32[1280]{0:T(1024)} %param.20) | copy-start | bytes 15364
  122.5 1.4 copy-start.1
  125.3 33.2 %copy-start.12 = (s32[64]{0:T(128)S(1)}, s32[64]{0:T(128)}, u32[]{:S(2)}) copy-start(s32[64]{0:T(128)} %param.23) | copy-start | bytes 772
  128.7 524.3 %all-gather.2.cloned.1.call-start = ((), (), s32[]{:S(2)}) async-start(), calls=%async_computation.3 | async-start | bytes 4227072 | tf_op jit(solution)/shard_map/all_gather | solution.py:93
Sparse Core Ops, SparseCore 0:
  67.6 54.8 all-reduce.2
  128.8 26.2 reduce-scatter.3
  158.2 85.5 all-gather.1
